TPU v7x, 256 devices: a whole 4x4x8 slice. The times are simulated.
256 devices in a mesh: pipe: 8 (over z_hi, x), expert: 32 (over y, z_lo, core).
Axes of the slice: x: 4, y: 4, z: 8 (z_hi: 2, z_lo: 4; z = z_hi * 4 + z_lo), core: 2. Of those that a mesh axis runs over, the one named last changes fastest.
Arguments:
- grad_out: bfloat16 [8, 4096, 2048], P('pipe', 'expert'), may hold values from -6 to 6
- expert_ids: int32 [8, 4096, 8], P('pipe', 'expert'), may hold values from 0 to 63, as said below
- slot_ids: int32 [8, 4096, 8], P('pipe', 'expert'), may hold values from 0 to 16, as said below
- gate_weights: float32 [8, 4096, 8], P('pipe', 'expert'), may hold values from 0.02 to 0.6
- saved_pre: bfloat16 [8, 64, 512, 1536], P('pipe', 'expert'), may hold values from -6 to 6
- down_weight: bfloat16 [8, 64, 768, 2048], P('pipe', 'expert'), may hold values from -0.21875 to 0.21875
- router_weight: bfloat16 [8, 64, 2048], P('pipe', 'expert'), may hold values from -0.125 to 0.125
Outputs:
- pre_grad: bfloat16 [8, 64, 512, 1536], P('pipe', 'expert')
- grad_inputs: bfloat16 [8, 4096, 2048], P('pipe', 'expert')
Inputs may be any that keep to these rules, and one draw needn't show every extreme that they name: `expert_ids`: each row names 8 different experts. `slot_ids`: for the pair (t, k): the number of earlier pairs (by row, then by k) among the same device's 128 rows of that section that name the same expert, capped at 16; the value 16 marks a pair that is dropped.
All inputs are finite; a program needn't handle non-finite values.
Results may differ from a plain program's by a relative error of at most 0.012.
Values may be sent and summed in bfloat16 or wider, within the bound.
No kernel may reach another device: no remote copies, remote signals or barrier semaphores. Data moves between devices by JAX's collectives and lax.ppermute only.
A program may use at most 128 MiB of HBM per device.

v0:
```python
import jax
import jax.numpy as jnp
from jax import lax
from jax.sharding import PartitionSpec as P


def passed_along(value, axis, by):
    peers = lax.axis_size(axis)
    return lax.ppermute(value, axis, [(i, (i + by) % peers) for i in range(peers)])


def per_device(grad_out, expert_ids, slot_ids, gate_weights, saved_pre, down_weight, router_weight):
    groups = lax.axis_size("expert")
    local_experts = down_weight.shape[1]
    hidden_width = down_weight.shape[2]
    tok_rows = grad_out.shape[1]
    width = grad_out.shape[2]
    top_count = expert_ids.shape[2]
    expert_total = local_experts * groups
    capacity = tok_rows * top_count // expert_total
    total_rows = expert_total * capacity
    features = grad_out[0]
    next_features = passed_along(features, "pipe", -1)
    next_router = passed_along(router_weight[0], "pipe", -1)
    route_ids = expert_ids[0]
    kept_pairs = slot_ids[0] < capacity
    destination = (
        route_ids % local_experts * (groups * capacity)
        + route_ids // local_experts * capacity
        + jnp.minimum(slot_ids[0], capacity - 1)
    )
    pair_dest = jnp.where(kept_pairs, destination, total_rows)
    row_ids = jnp.arange(total_rows, dtype=jnp.int32)
    token_hit = pair_dest[None, :, :] == row_ids[:, None, None]
    token_onehot = jnp.any(token_hit, axis=2).astype(jnp.bfloat16)
    token_rows = jnp.dot(token_onehot, features, preferred_element_type=jnp.float32).astype(
        jnp.bfloat16
    )
    matches = token_hit.reshape(total_rows, tok_rows * top_count)
    gate_low = gate_weights[0].astype(jnp.bfloat16)
    slot_gate = jnp.sum(
        jnp.where(matches, gate_low.reshape(-1).astype(jnp.float32)[None, :], jnp.float32(0.0)),
        axis=1,
    )
    arrived = lax.all_to_all(
        token_rows.reshape(local_experts, groups, capacity, -1),
        "expert",
        split_axis=1,
        concat_axis=1,
        tiled=True,
    )
    me = lax.axis_index("expert")
    gate_table = (
        slot_gate.reshape(local_experts, groups, capacity)
        .transpose(1, 0, 2)
        .reshape(1, total_rows)
        .astype(jnp.bfloat16)
    )
    own_block = jnp.concatenate([gate_table, next_router.reshape(1, local_experts * width)], axis=1)
    blocks = lax.dynamic_update_slice(
        jnp.zeros((groups, own_block.shape[1]), jnp.bfloat16), own_block, (me, 0)
    )
    gathered = lax.psum(blocks, "expert")
    gate_in = (
        lax.dynamic_slice_in_dim(
            gathered[:, :total_rows],
            me * local_experts * capacity,
            local_experts * capacity,
            axis=1,
        )
        .reshape(groups, local_experts, capacity)
        .transpose(1, 0, 2)
        .reshape(local_experts, groups * capacity)
        .astype(jnp.float32)
    )
    next_router_full = gathered[:, total_rows:].reshape(expert_total, width)
    rows_in = arrived.reshape(local_experts, groups * capacity, -1).astype(jnp.float32)
    pre_saved = saved_pre[0]
    gate_part = pre_saved[..., :hidden_width].astype(jnp.float32)
    up_part = pre_saved[..., hidden_width:].astype(jnp.float32)
    sigmoid_gate = jax.nn.sigmoid(gate_part)
    silu_gate = gate_part * sigmoid_gate
    hidden = (silu_gate * up_part).astype(jnp.bfloat16)
    weights = down_weight[0]
    expert_out = jnp.einsum(
        "jsf,jfd->jsd", hidden, weights, preferred_element_type=jnp.float32
    ).astype(jnp.bfloat16)
    row_scores = jnp.sum(
        rows_in * lax.optimization_barrier(expert_out).astype(jnp.float32), axis=-1
    )
    returned = lax.all_to_all(
        row_scores.reshape(local_experts, groups, capacity),
        "expert",
        split_axis=1,
        concat_axis=1,
        tiled=True,
    )
    pair_scores = jnp.sum(
        jnp.where(matches, returned.reshape(total_rows)[:, None], jnp.float32(0.0)), axis=0
    ).reshape(tok_rows, top_count)
    scaled_rows = (gate_in[..., None] * rows_in).astype(jnp.bfloat16)
    row_grad = jnp.einsum("jsd,jfd->jsf", scaled_rows, weights, preferred_element_type=jnp.float32)
    gate_grad = row_grad * up_part * sigmoid_gate * (1.0 + gate_part * (1.0 - sigmoid_gate))
    up_grad = row_grad * silu_gate
    pre_grad = jnp.concatenate([gate_grad, up_grad], axis=-1).astype(jnp.bfloat16)
    gate_values = gate_weights[0]
    weighted_sum = jnp.sum(gate_values * pair_scores, axis=-1, keepdims=True)
    select_grad = gate_values * (pair_scores - weighted_sum)
    expert_columns = jnp.arange(expert_total, dtype=jnp.int32)
    chosen = route_ids[:, :, None] == expert_columns[None, None, :]
    logit_grad = jnp.sum(
        jnp.where(chosen, select_grad[:, :, None], jnp.float32(0.0)), axis=1
    ).astype(jnp.bfloat16)
    next_logit_grad = passed_along(logit_grad, "pipe", -1)
    router_part = jnp.dot(next_logit_grad, next_router_full, preferred_element_type=jnp.float32)
    outgoing = (next_features.astype(jnp.float32) + router_part).astype(jnp.bfloat16)
    return (pre_grad[None], outgoing[None])


def solution(mesh):
    in_specs = (
        P("pipe", "expert", None),
        P("pipe", "expert", None),
        P("pipe", "expert", None),
        P("pipe", "expert", None),
        P("pipe", "expert", None, None),
        P("pipe", "expert", None, None),
        P("pipe", "expert", None),
    )
    out_specs = (P("pipe", "expert", None, None), P("pipe", "expert", None))
    return jax.shard_map(
        per_device, mesh=mesh, in_specs=in_specs, out_specs=out_specs, check_vma=False
    )
```

profile of v0, /device:TPU:1, one launch (start us, length us, event | category | flops | bytes accessed | tf_op | source)
XLA Modules:
  0.0 472.0 jit_solution(9623698709281325380)
XLA Ops:
  7.2 0.7 fusion.27
  7.9 1.9 fusion.6
  9.8 2.3 convolution_convert_fusion
  12.1 2.3 copy.47
  14.4 10.4 %all-to-all-start = ((bf16[2,32,16,2048]{3,2,0,1:T(8,128)(2,1)}), bf16[2,32,16,2048]{3,2,0,1:T(8,128)(2,1)}, u32[]{:S(2)}, u32[]{:S(2)}) async-start(bf16[2,32,16,2048]{3,2,0,1:T(8,128)(2,1)} %copy.47), calls=%async_computation | async-start | bytes 8388608 | tf_op jit(solution)/shard_map/all_to_all | solution.py:45
  24.8 6.5 %collective-permute-start = (bf16[2,2048]{1,0:T(2,128)(2,1)S(1)}, bf16[2,2048]{1,0:T(2,128)(2,1)S(1)}, u32[]{:S(2)}, u32[]{:S(2)}) collective-permute-start(bf16[2,2048]{1,0:T(2,128)(2,1)S(1)} %bitcast.57), channel_id=1, source_target_pairs={{0,224},{32,0},{64,32},{96,64},{128,96},{160,128},{192,160},{224,1... | collective-permute-start | bytes 24584 | tf_op jit(solution)/shard_map/ppermute | solution.py:9
  31.8 9.3 %fusion.7 = bf16[2,512,2048]{2,1,0:T(8,128)(2,1)} fusion(bf16[1,2,768,2048]{3,2,1,0:T(8,128)(2,1)} %param.12, bf16[2,512,1536]{2,1,0:T(8,128)(2,1)} %bitcast.55), kind=kOutput, calls=%fused_computation.18 | convolution fusion | flops 3229614080 | bytes 13631488 | tf_op jit(solution)/shard_map/jsf,jfd->jsd/dot_general | solution.py:85
  41.1 101.0 %all-to-all-done = bf16[2,32,16,2048]{3,2,0,1:T(8,128)(2,1)} async-done(((bf16[2,32,16,2048]{3,2,0,1:T(8,128)(2,1)}), bf16[2,32,16,2048]{3,2,0,1:T(8,128)(2,1)}, u32[]{:S(2)}, u32[]{:S(2)}) %all-to-all-start) | async-done | bytes 4194336 | tf_op jit(solution)/shard_map/all_to_all | solution.py:45
  142.1 3.4 copy.48
  145.5 3.2 copy-done
  148.7 0.9 fusion.1
  149.7 0.6 copy.50
  150.3 4.7 all-to-all-start.1
  155.8 6.8 %all-to-all-done.1 = f32[2,32,16]{2,0,1:T(2,128)S(1)} async-done(((f32[2,32,16]{2,0,1:T(2,128)}), f32[2,32,16]{2,0,1:T(2,128)S(1)}, u32[]{:S(2)}, u32[]{:S(2)}) %all-to-all-start.1) | async-done | bytes 4128 | tf_op jit(solution)/shard_map/all_to_all | solution.py:91
  162.7 1.2 select_reduce_fusion
  164.1 0.6 copy.45
  164.9 4.8 %dynamic_update_slice.3 = bf16[32,5120]{0,1:T(8,128)(2,1)S(1)} dynamic-update-slice(bf16[32,5120]{0,1:T(8,128)(2,1)S(1)} %broadcast_in_dim.54, bf16[1,5120]{0,1:T(8,128)(2,1)S(1)} %copy.45, s32[]{:T(128)S(6)} %select_n.41, s32[]{:T(128)} %constant.39.clone.1) | dynamic-update-slice | bytes 20484 | tf_op jit(solution)/shard_map/dynamic_update_slice | solution.py:60
  169.7 1.0 copy-done.1
  171.2 276.7 %all-reduce.2.cloned.1.call-done = bf16[32,5120]{0,1:T(8,128)(2,1)} async-done(((bf16[32,5120]{0,1:T(8,128)(2,1)}), bf16[32,5120]{0,1:T(8,128)(2,1)}) %all-reduce.2.cloned.1.call-update) | async-done | bytes 327696 | tf_op jit(solution)/shard_map/psum | solution.py:63
  447.9 1.0 slice.16
  449.1 4.0 fusion
  453.3 7.3 %fusion.20 = (bf16[1,2,512,768]{3,2,1,0:T(8,128)(2,1)S(1)}, bf16[1,2,512,768]{3,2,1,0:T(8,128)(2,1)S(1)}) fusion(bf16[2,512,1536]{2,1,0:T(8,128)(2,1)S(1)} %bitcast.56, bf16[2,512,2048]{2,1,0:T(8,128)(2,1)S(1)} %fusion, bf16[1,2,768,2048]{3,2,1,0:T(8,128)(2,1)} %param.12), kind=kOutput, calls=%fused_computation.31 | convolution fusion | flops 3233021952 | bytes 16777216 | tf_op jit(solution)/shard_map/jsd,jfd->jsf/dot_general | solution.py:102
  460.6 1.9 pad_maximum_fusion
  463.0 2.2 fusion.22
  (49 shorter events, 3.2 us)
Async XLA Ops:
  14.4 10.4 %copy-start.7 = (bf16[1,2,2048]{2,1,0:T(2,128)(2,1)S(1)}, bf16[1,2,2048]{2,1,0:T(2,128)(2,1)}, u32[]{:S(2)}) copy-start(bf16[1,2,2048]{2,1,0:T(2,128)(2,1)} %param.13) | copy-start | bytes 24580
  14.4 16.9 %copy-start.3 = (bf16[1,128,2048]{2,1,0:T(8,128)(2,1)S(1)}, bf16[1,128,2048]{2,1,0:T(8,128)(2,1)}, u32[]{:S(2)}) copy-start(bf16[1,128,2048]{2,1,0:T(8,128)(2,1)} %param.7) | copy-start | bytes 1572868
  14.4 127.7 %all-to-all-start = ((bf16[2,32,16,2048]{3,2,0,1:T(8,128)(2,1)}), bf16[2,32,16,2048]{3,2,0,1:T(8,128)(2,1)}, u32[]{:S(2)}, u32[]{:S(2)}) async-start(bf16[2,32,16,2048]{3,2,0,1:T(8,128)(2,1)} %copy.47), calls=%async_computation | async-start | bytes 8388608 | tf_op jit(solution)/shard_map/all_to_all | solution.py:45
  24.8 131.0 %collective-permute-start = (bf16[2,2048]{1,0:T(2,128)(2,1)S(1)}, bf16[2,2048]{1,0:T(2,128)(2,1)S(1)}, u32[]{:S(2)}, u32[]{:S(2)}) collective-permute-start(bf16[2,2048]{1,0:T(2,128)(2,1)S(1)} %bitcast.57), channel_id=1, source_target_pairs={{0,224},{32,0},{64,32},{96,64},{128,96},{160,128},{192,160},{224,1... | collective-permute-start | bytes 24584 | tf_op jit(solution)/shard_map/ppermute | solution.py:9
  31.2 431.7 %collective-permute-start.1 = (bf16[128,2048]{1,0:T(8,128)(2,1)S(1)}, bf16[128,2048]{1,0:T(8,128)(2,1)}, u32[]{:S(2)}, u32[]{:S(2)}) collective-permute-start(bf16[128,2048]{1,0:T(8,128)(2,1)S(1)} %bitcast.48), channel_id=1, source_target_pairs={{0,224},{32,0},{64,32},{96,64},{128,96},{160,128},{192,160},{224,1... | collective-permute-start | bytes 1572872 | tf_op jit(solution)/shard_map/ppermute | solution.py:9
  142.1 6.6 %copy-start.2 = (bf16[2,512,2048]{2,1,0:T(8,128)(2,1)S(1)}, bf16[2,512,2048]{2,1,0:T(8,128)(2,1)}, u32[]{:S(2)}) copy-start(bf16[2,512,2048]{2,1,0:T(8,128)(2,1)} %fusion.7) | copy-start | bytes 12582916
  145.5 3.2 copy-start
  148.7 6.6 %copy-start.4 = (f32[1,128,8]{1,2,0:T(8,128)S(1)}, f32[1,128,8]{1,2,0:T(8,128)}, u32[]{:S(2)}) copy-start(f32[1,128,8]{1,2,0:T(8,128)} %param.10) | copy-start | bytes 12292
  150.3 12.3 %all-to-all-start.1 = ((f32[2,32,16]{2,0,1:T(2,128)}), f32[2,32,16]{2,0,1:T(2,128)S(1)}, u32[]{:S(2)}, u32[]{:S(2)}) async-start(f32[2,32,16]{2,0,1:T(2,128)} %copy.50), calls=%async_computation.1 | async-start | bytes 65536 | tf_op jit(solution)/shard_map/all_to_all | solution.py:91
  155.0 292.9 %all-reduce.2.cloned.1.call-start = ((), (), s32[]{:S(2)}) async-start(), calls=%async_computation.2 | async-start | bytes 2621440 | tf_op jit(solution)/shard_map/psum | solution.py:63
  164.7 6.4 %copy-start.5 = (s32[1,128,8]{1,2,0:T(8,128)S(1)}, s32[1,128,8]{1,2,0:T(8,128)}, u32[]{:S(2)}) copy-start(s32[1,128,8]{1,2,0:T(8,128)} %param.8) | copy-start | bytes 12292
  169.6 1.1 copy-start.1
  171.1 291.8 %collective-permute-start.2 = (bf16[128,64]{0,1:T(8,128)(2,1)S(1)}, bf16[128,64]{0,1:T(8,128)(2,1)S(1)}, u32[]{:S(2)}, u32[]{:S(2)}) collective-permute-start(bf16[128,64]{0,1:T(8,128)(2,1)S(1)} %select_reduce_fusion.2), channel_id=1, source_target_pairs={{0,224},{32,0},{64,32},{96,64},{128,96},{160,128},{192,160},{224,1... | collective-permute-start | bytes 49160 | tf_op jit(solution)/shard_map/ppermute | solution.py:9
  449.1 4.3 copy-start.6
  460.6 1.9 slice-start
Sparse Core Ops, SparseCore 0:
  170.8 276.9 all-reduce.1
where the time goes:
time: 472 us
  waiting for transfers between devices  384 us (81%)
  starting transfers between devices  22.4 us (5%)
  matrix products  21 us (4%)
  local copies, waits for them, and re-layouts  18.9 us (4%)
  between operations  14.3 us (3%)
  other arithmetic  10.9 us (2%)
    psum x1, waiting for transfers between devices, per_device(): gathered = lax.psum(blocks, 'expert')  277 us
    all_to_all x1, waiting for transfers between devices, per_device(): lax.all_to_all(token_rows.reshape(local_experts, groups, capacity, -1), '...  101 us
    all_to_all x1, starting transfers between devices, per_device(): lax.all_to_all(token_rows.reshape(local_experts, groups, capacity, -1), '...  10.4 us
  transfers between devices with their start and end apart: 6, of which 3 were waited for; matrix products, arithmetic and copies ran while one was open for 8% of the time, Pallas kernels for 0%

commit v1 on v0

--- a/solution.py
+++ b/solution.py
@@ -2,6 +2,7 @@
 import jax.numpy as jnp
 from jax import lax
 from jax.sharding import PartitionSpec as P
+from jax.lax import all_gather
 
 
 def passed_along(value, axis, by):
@@ -60,7 +61,8 @@
     blocks = lax.dynamic_update_slice(
         jnp.zeros((groups, own_block.shape[1]), jnp.bfloat16), own_block, (me, 0)
     )
-    gathered = lax.psum(blocks, "expert")
+    e_now = all_gather(blocks, "expert")
+    gathered = jnp.sum(e_now, axis=0)
     gate_in = (
         lax.dynamic_slice_in_dim(
             gathered[:, :total_rows],

time: 472 us -> 258 us (0.55)
  waiting for transfers between devices: 384 us -> 165 us
  local copies, waits for them, and re-layouts: 18.9 us -> 12.3 us
  other arithmetic: 10.9 us -> 17.3 us
  starting transfers between devices: 22.4 us -> 28.5 us
    psum x1 -> x0, waiting for transfers between devices: 277 us -> none  [per_device(): gathered = lax.psum(blocks, 'expert')]
    all_gather x0 -> x1, waiting for transfers between devices: none -> 79.3 us  [per_device(): e_now = all_gather(blocks, 'expert')]
    all_to_all x1, waiting for transfers between devices: 101 us -> 79.1 us  [per_device(): lax.all_to_all(token_rows.reshape(local_experts, groups, capacity, -1), '...]
    ppermute x3, starting transfers between devices: 7.11 us -> 13.4 us  [passed_along(): lax.ppermute(value, axis, [(i, (i + by) % peers) for i in range(peers)])]
    reduce_sum x0 -> x1, other arithmetic: none -> 6.24 us  [per_device(): gathered = jnp.sum(e_now, axis=0)]
  transfers between devices with their start and end apart: 6 -> 6, of which waited for: 3 -> 3; matrix products, arithmetic and copies ran while one was open for 8% -> 14% of each run, Pallas kernels for 0% -> 0%
where the time goes in v1:
time: 258 us
  waiting for transfers between devices  165 us (64%)
  starting transfers between devices  28.5 us (11%)
  matrix products  20 us (8%)
  other arithmetic  17.3 us (7%)
  between operations  14.3 us (6%)
  local copies, waits for them, and re-layouts  12.3 us (5%)
    all_gather x1, waiting for transfers between devices, per_device(): e_now = all_gather(blocks, 'expert')  79.3 us
    all_to_all x1, waiting for transfers between devices, per_device(): lax.all_to_all(token_rows.reshape(local_experts, groups, capacity, -1), '...  79.1 us
    ppermute x3, starting transfers between devices, passed_along(): lax.ppermute(value, axis, [(i, (i + by) % peers) for i in range(peers)])  13.4 us
    all_to_all x1, starting transfers between devices, per_device(): lax.all_to_all(token_rows.reshape(local_experts, groups, capacity, -1), '...  10.4 us
    dot_general x1, matrix products, per_device(): jnp.einsum('jsf,jfd->jsd', hidden, weights, preferred_element_type=jnp.fl...  9.29 us
    dot_general x1, matrix products, per_device(): jnp.einsum('jsd,jfd->jsf', scaled_rows, weights, preferred_element_type=j...  7.27 us
    all_to_all x1, waiting for transfers between devices, per_device(): lax.all_to_all(row_scores.reshape(local_experts, groups, capacity), 'expe...  7.06 us
    reduce_sum x1, other arithmetic, per_device(): gathered = jnp.sum(e_now, axis=0)  6.24 us
  transfers between devices with their start and end apart: 6, of which 3 were waited for; matrix products, arithmetic and copies ran while one was open for 14% of the time, Pallas kernels for 0%

profile of v1, /device:TPU:1, one launch (start us, length us, event | category | flops | bytes accessed | tf_op | source)
XLA Modules:
  0.0 257.7 jit_solution(5954739009737398312)
XLA Ops:
  7.2 0.7 fusion.27
  7.9 1.9 fusion.6
  9.8 2.3 convolution_convert_fusion
  12.1 2.3 copy.56
  14.4 10.4 %all-to-all-start = ((bf16[2,32,16,2048]{3,2,0,1:T(8,128)(2,1)}), bf16[2,32,16,2048]{3,2,0,1:T(8,128)(2,1)}, u32[]{:S(2)}, u32[]{:S(2)}) async-start(bf16[2,32,16,2048]{3,2,0,1:T(8,128)(2,1)} %copy.56), calls=%async_computation | async-start | bytes 8388608 | tf_op jit(solution)/shard_map/all_to_all | solution.py:46
  24.8 6.5 %collective-permute-start = (bf16[2,2048]{1,0:T(2,128)(2,1)S(1)}, bf16[2,2048]{1,0:T(2,128)(2,1)S(1)}, u32[]{:S(2)}, u32[]{:S(2)}) collective-permute-start(bf16[2,2048]{1,0:T(2,128)(2,1)S(1)} %bitcast.58), channel_id=1, source_target_pairs={{0,224},{32,0},{64,32},{96,64},{128,96},{160,128},{192,160},{224,1... | collective-permute-start | bytes 24584 | tf_op jit(solution)/shard_map/ppermute | solution.py:10
  31.3 9.3 %fusion.7 = bf16[2,512,2048]{2,1,0:T(8,128)(2,1)} fusion(bf16[1,2,768,2048]{3,2,1,0:T(8,128)(2,1)} %param.12, bf16[2,512,1536]{2,1,0:T(8,128)(2,1)} %bitcast.56), kind=kOutput, calls=%fused_computation.18 | convolution fusion | flops 3229614080 | bytes 13631488 | tf_op jit(solution)/shard_map/jsf,jfd->jsd/dot_general | solution.py:87
  40.6 79.1 %all-to-all-done = bf16[2,32,16,2048]{3,2,0,1:T(8,128)(2,1)} async-done(((bf16[2,32,16,2048]{3,2,0,1:T(8,128)(2,1)}), bf16[2,32,16,2048]{3,2,0,1:T(8,128)(2,1)}, u32[]{:S(2)}, u32[]{:S(2)}) %all-to-all-start) | async-done | bytes 4194336 | tf_op jit(solution)/shard_map/all_to_all | solution.py:46
  119.6 3.4 %copy.57 = f32[2,32,16,2048]{3,2,1,0:T(8,128)S(1)} copy(bf16[2,32,16,2048]{3,2,0,1:T(8,128)(2,1)} %all-to-all-done) | data formatting | bytes 12582912 | tf_op jit(solution)/shard_map/convert_element_type | solution.py:79
  123.0 3.3 %copy-done = f32[2,32,16,2048]{3,2,1,0:T(8,128)} copy-done((f32[2,32,16,2048]{3,2,1,0:T(8,128)}, f32[2,32,16,2048]{3,2,1,0:T(8,128)S(1)}, u32[]{:S(2)}) %copy-start) | copy-done | bytes 8388632
  126.4 0.9 fusion.1
  127.4 0.6 copy.59
  128.0 4.7 %all-to-all-start.1 = ((f32[2,32,16]{2,0,1:T(2,128)}), f32[2,32,16]{2,0,1:T(2,128)S(1)}, u32[]{:S(2)}, u32[]{:S(2)}) async-start(f32[2,32,16]{2,0,1:T(2,128)} %copy.59), calls=%async_computation.1 | async-start | bytes 65536 | tf_op jit(solution)/shard_map/all_to_all | solution.py:93
  133.2 7.1 %all-to-all-done.1 = f32[2,32,16]{2,0,1:T(2,128)S(1)} async-done(((f32[2,32,16]{2,0,1:T(2,128)}), f32[2,32,16]{2,0,1:T(2,128)S(1)}, u32[]{:S(2)}, u32[]{:S(2)}) %all-to-all-start.1) | async-done | bytes 4128 | tf_op jit(solution)/shard_map/all_to_all | solution.py:93
  140.3 1.2 select_reduce_fusion
  142.1 0.7 copy-done.2
  142.9 6.3 %collective-permute-start.1 = (bf16[128,2048]{1,0:T(8,128)(2,1)S(1)}, bf16[128,2048]{1,0:T(8,128)(2,1)S(1)}, u32[]{:S(2)}, u32[]{:S(2)}) collective-permute-start(bf16[128,2048]{1,0:T(8,128)(2,1)S(1)} %bitcast.49), channel_id=1, source_target_pairs={{0,224},{32,0},{64,32},{96,64},{128,96},{160,128},{192,160},{224,1... | collective-permute-start | bytes 1572872 | tf_op jit(solution)/shard_map/ppermute | solution.py:10
  149.7 0.6 collective-permute-start.2
  150.3 79.3 %all-gather.2.cloned.1.call-done = bf16[32,32,5120]{2,1,0:T(8,128)(2,1)} async-done(((bf16[1,32,5120]{2,1,0:T(8,128)(2,1)}), bf16[32,32,5120]{2,1,0:T(8,128)(2,1)}) %all-gather.2.cloned.1.call-update) | async-done | bytes 10485776 | tf_op jit(solution)/shard_map/all_gather | solution.py:64
  229.6 6.2 %reduce_sum.58 = bf16[32,5120]{1,0:T(8,128)(2,1)S(1)} reduce(bf16[32,32,5120]{2,1,0:T(8,128)(2,1)} %all-gather.2.cloned.1.call-done, bf16[]{:T(256)} %constant.39.clone.1), dimensions={0}, to_apply=%region_1.2 | reduce | flops 5079040 | bytes 10813442 | tf_op jit(solution)/shard_map/reduce_sum | solution.py:65
  236.2 4.0 %fusion = bf16[2,512,2048]{2,1,0:T(8,128)(2,1)S(1)} fusion(f32[2,32,16,2048]{3,2,1,0:T(8,128)} %copy-done, f32[2,512]{1,0:T(2,128)S(1)} %reshape.129), kind=kLoop, calls=%fused_computation.2 | loop fusion | flops 4194304 | bytes 12587008 | tf_op jit(solution)/shard_map/convert_element_type | solution.py:103
  240.4 7.3 %fusion.20 = (bf16[1,2,512,768]{3,2,1,0:T(8,128)(2,1)S(1)}, bf16[1,2,512,768]{3,2,1,0:T(8,128)(2,1)S(1)}) fusion(bf16[2,512,1536]{2,1,0:T(8,128)(2,1)S(1)} %bitcast.57, bf16[2,512,2048]{2,1,0:T(8,128)(2,1)S(1)} %fusion, bf16[1,2,768,2048]{3,2,1,0:T(8,128)(2,1)} %param.12), kind=kOutput, calls=%fused_computation.31 | convolution fusion | flops 3233021952 | bytes 16777216 | tf_op jit(solution)/shard_map/jsd,jfd->jsf/dot_general | solution.py:104
  247.7 1.9 pad_maximum_fusion
  249.8 1.1 fusion.22
  (47 shorter events, 2.3 us)
Async XLA Ops:
  14.4 10.4 %copy-start.7 = (bf16[1,2,2048]{2,1,0:T(2,128)(2,1)S(1)}, bf16[1,2,2048]{2,1,0:T(2,128)(2,1)}, u32[]{:S(2)}) copy-start(bf16[1,2,2048]{2,1,0:T(2,128)(2,1)} %param.13) | copy-start | bytes 24580
  14.4 105.2 %all-to-all-start = ((bf16[2,32,16,2048]{3,2,0,1:T(8,128)(2,1)}), bf16[2,32,16,2048]{3,2,0,1:T(8,128)(2,1)}, u32[]{:S(2)}, u32[]{:S(2)}) async-start(bf16[2,32,16,2048]{3,2,0,1:T(8,128)(2,1)} %copy.56), calls=%async_computation | async-start | bytes 8388608 | tf_op jit(solution)/shard_map/all_to_all | solution.py:46
  24.8 108.4 %collective-permute-start = (bf16[2,2048]{1,0:T(2,128)(2,1)S(1)}, bf16[2,2048]{1,0:T(2,128)(2,1)S(1)}, u32[]{:S(2)}, u32[]{:S(2)}) collective-permute-start(bf16[2,2048]{1,0:T(2,128)(2,1)S(1)} %bitcast.58), channel_id=1, source_target_pairs={{0,224},{32,0},{64,32},{96,64},{128,96},{160,128},{192,160},{224,1... | collective-permute-start | bytes 24584 | tf_op jit(solution)/shard_map/ppermute | solution.py:10
  119.6 6.7 %copy-start.1 = (bf16[2,512,2048]{2,1,0:T(8,128)(2,1)S(1)}, bf16[2,512,2048]{2,1,0:T(8,128)(2,1)}, u32[]{:S(2)}) copy-start(bf16[2,512,2048]{2,1,0:T(8,128)(2,1)} %fusion.7) | copy-start | bytes 12582916
  123.0 3.3 %copy-start = (f32[2,32,16,2048]{3,2,1,0:T(8,128)}, f32[2,32,16,2048]{3,2,1,0:T(8,128)S(1)}, u32[]{:S(2)}) copy-start(f32[2,32,16,2048]{3,2,1,0:T(8,128)S(1)} %copy.57) | copy-start | bytes 25165828
  126.4 6.4 %copy-start.4 = (f32[1,128,8]{1,2,0:T(8,128)S(1)}, f32[1,128,8]{1,2,0:T(8,128)}, u32[]{:S(2)}) copy-start(f32[1,128,8]{1,2,0:T(8,128)} %param.10) | copy-start | bytes 12292
  126.4 16.5 %copy-start.3 = (bf16[1,128,2048]{2,1,0:T(8,128)(2,1)S(1)}, bf16[1,128,2048]{2,1,0:T(8,128)(2,1)}, u32[]{:S(2)}) copy-start(bf16[1,128,2048]{2,1,0:T(8,128)(2,1)} %param.7) | copy-start | bytes 1572868
  126.4 23.2 %copy-start.5 = (s32[1,128,8]{1,2,0:T(8,128)S(1)}, s32[1,128,8]{1,2,0:T(8,128)}, u32[]{:S(2)}) copy-start(s32[1,128,8]{1,2,0:T(8,128)} %param.8) | copy-start | bytes 12292
  128.0 12.3 %all-to-all-start.1 = ((f32[2,32,16]{2,0,1:T(2,128)}), f32[2,32,16]{2,0,1:T(2,128)S(1)}, u32[]{:S(2)}, u32[]{:S(2)}) async-start(f32[2,32,16]{2,0,1:T(2,128)} %copy.59), calls=%async_computation.1 | async-start | bytes 65536 | tf_op jit(solution)/shard_map/all_to_all | solution.py:93
  132.7 96.9 %all-gather.2.cloned.1.call-start = ((), (), s32[]{:S(2)}) async-start(), calls=%async_computation.2 | async-start | bytes 10813440 | tf_op jit(solution)/shard_map/all_gather | solution.py:64
  142.1 0.7 copy-start.2
  142.9 106.9 %collective-permute-start.1 = (bf16[128,2048]{1,0:T(8,128)(2,1)S(1)}, bf16[128,2048]{1,0:T(8,128)(2,1)S(1)}, u32[]{:S(2)}, u32[]{:S(2)}) collective-permute-start(bf16[128,2048]{1,0:T(8,128)(2,1)S(1)} %bitcast.49), channel_id=1, source_target_pairs={{0,224},{32,0},{64,32},{96,64},{128,96},{160,128},{192,160},{224,1... | collective-permute-start | bytes 1572872 | tf_op jit(solution)/shard_map/ppermute | solution.py:10
  149.7 100.1 %collective-permute-start.2 = (bf16[128,64]{0,1:T(8,128)(2,1)S(1)}, bf16[128,64]{0,1:T(8,128)(2,1)S(1)}, u32[]{:S(2)}, u32[]{:S(2)}) collective-permute-start(bf16[128,64]{0,1:T(8,128)(2,1)S(1)} %select_reduce_fusion.2), channel_id=1, source_target_pairs={{0,224},{32,0},{64,32},{96,64},{128,96},{160,128},{192,160},{224,1... | collective-permute-start | bytes 49160 | tf_op jit(solution)/shard_map/ppermute | solution.py:10
  236.2 4.3 %copy-start.6 = (bf16[1,2,512,1536]{3,2,1,0:T(8,128)(2,1)S(1)}, bf16[1,2,512,1536]{3,2,1,0:T(8,128)(2,1)}, u32[]{:S(2)}) copy-start(bf16[1,2,512,1536]{3,2,1,0:T(8,128)(2,1)} %param.11) | copy-start | bytes 9437188
Sparse Core Ops, SparseCore 0:
  143.0 86.5 all-gather.1
